TPU v7x, 32 devices: a whole 2x2x4 slice. The times are simulated.
32 devices in a mesh: blk: 4 (over y, x), group: 8 (over z, core).
Axes of the slice: x: 2, y: 2, z: 4, core: 2. Of those that a mesh axis runs over, the one named last changes fastest.
Arguments:
- picture_vector_list: bfloat16 [8, 1024, 768], P('group', 'blk'), may hold values from -0.25 to 0.25
- caption_latent_matrix: bfloat16 [8, 1024, 3072], P('group', 'blk'), may hold values from -6 to 6
- linear_map_matrix: bfloat16 [3072, 768], P('group'), may hold values from -0.109375 to 0.109375
- target_match_index: int32 [8, 1024], P('group', 'blk'), may hold values from 0 to 1023, each once within a row
- sharpness_factor: float32 [1], replicated, may hold values from 24 to 40
- offset_term: float32 [1], replicated, may hold values from -6 to -5
Outputs:
- row_loss: float32 [8, 1024], P('group', 'blk')
- image_grad: bfloat16 [8, 1024, 768], P('group', 'blk')
- projection_grad: float32 [3072, 768], P(('blk', 'group'))
Inputs may be any that keep to these rules, and one draw needn't show every extreme that they name: `target_match_index`: each data group's row of positives is a permutation of 0 to 1023.
All inputs are finite; a program needn't handle non-finite values.
Results may differ from a plain program's by a relative error of at most 0.015.
Values may be sent and summed in bfloat16 or wider, within the bound.
No kernel may reach another device: no remote copies, remote signals or barrier semaphores. Data moves between devices by JAX's collectives and lax.ppermute only.
A program may use at most 64 MiB of HBM per device.

v0:
```python
import jax
import jax.numpy as jnp
from jax import lax
from jax.sharding import PartitionSpec as P

epsilon = 1e-06


def body(
    picture_vector_list,
    caption_latent_matrix,
    linear_map_matrix,
    target_match_index,
    sharpness_factor,
    offset_term,
):
    image_rows = picture_vector_list[0]
    hidden_rows = caption_latent_matrix[0]
    label_rows = target_match_index[0]
    row_count = image_rows.shape[0]
    blocks = lax.axis_size("blk")
    my_index = lax.axis_index("blk")
    multiplier_amount = sharpness_factor[0]
    offset_value = offset_term[0]
    piece_rows = linear_map_matrix.shape[0] // blocks
    w_piece = lax.dynamic_slice_in_dim(linear_map_matrix, my_index * piece_rows, piece_rows, 0)
    w_full = lax.all_gather(w_piece, ("group", "blk"), axis=0, tiled=True)
    hidden_chunk = lax.all_to_all(hidden_rows, "blk", split_axis=1, concat_axis=0, tiled=True)
    image_float = image_rows.astype(jnp.float32)
    image_scale = lax.rsqrt(jnp.sum(image_float * image_float, axis=1, keepdims=True) + epsilon)
    image_dir = image_float * image_scale
    image_unit = image_dir.astype(jnp.bfloat16)
    projected = jnp.dot(hidden_rows, w_full, preferred_element_type=jnp.float32)
    text_scale = lax.rsqrt(jnp.sum(projected * projected, axis=1, keepdims=True) + epsilon)
    text_dir = projected * text_scale
    text_unit = text_dir.astype(jnp.bfloat16)
    both = lax.all_gather(jnp.stack([image_unit, text_unit]), "blk", axis=1, tiled=True)
    image_all = both[0]
    text_all = both[1]
    label_all = lax.all_gather(label_rows.astype(jnp.float32), "blk", axis=0, tiled=True)

    def weights_of(logits, pair_sign):
        return (-pair_sign * jax.nn.sigmoid(-pair_sign * logits) * multiplier_amount).astype(
            jnp.bfloat16
        )

    scores = lax.dot_general(
        image_unit, text_all, (((1,), (1,)), ((), ())), preferred_element_type=jnp.float32
    )
    logits = multiplier_amount * scores + offset_value
    text_columns = jnp.arange(text_all.shape[0], dtype=jnp.int32)
    pair_sign = jnp.where(label_rows[:, None] == text_columns[None, :], 1.0, -1.0).astype(
        jnp.float32
    )
    loss_local = -jnp.sum(jax.nn.log_sigmoid(pair_sign * logits), axis=1)
    image_unit_grad = jnp.dot(
        weights_of(logits, pair_sign), text_all, preferred_element_type=jnp.float32
    )
    scores_t = lax.dot_general(
        image_all, text_unit, (((1,), (1,)), ((), ())), preferred_element_type=jnp.float32
    )
    logits_t = multiplier_amount * scores_t + offset_value
    own_columns = (my_index * row_count + jnp.arange(row_count, dtype=jnp.int32)).astype(
        jnp.float32
    )
    pair_sign_t = jnp.where(label_all[:, None] == own_columns[None, :], 1.0, -1.0).astype(
        jnp.float32
    )
    text_unit_grad = lax.dot_general(
        weights_of(logits_t, pair_sign_t),
        image_all,
        (((0,), (0,)), ((), ())),
        preferred_element_type=jnp.float32,
    )
    image_grad = (
        image_scale
        * (
            image_unit_grad
            - image_dir * jnp.sum(image_dir * image_unit_grad, axis=1, keepdims=True)
        )
    ).astype(jnp.bfloat16)
    projection_output_gradient = (
        text_scale
        * (text_unit_grad - text_dir * jnp.sum(text_dir * text_unit_grad, axis=1, keepdims=True))
    ).astype(jnp.bfloat16)
    grad_all = lax.all_gather(projection_output_gradient, "blk", axis=0, tiled=True)
    partial = lax.dot_general(
        hidden_chunk, grad_all, (((0,), (0,)), ((), ())), preferred_element_type=jnp.float32
    )
    projection_grad = lax.psum_scatter(partial, "group", scatter_dimension=0, tiled=True)
    return (loss_local[None], image_grad[None], projection_grad)


def solution(mesh):
    return jax.shard_map(
        body,
        mesh=mesh,
        in_specs=(
            P("group", "blk", None),
            P("group", "blk", None),
            P("group", None),
            P("group", "blk"),
            P(),
            P(),
        ),
        out_specs=(P("group", "blk"), P("group", "blk", None), P(("blk", "group"), None)),
        check_vma=False,
    )
```

profile of v0, /device:TPU:0, one launch (start us, length us, event | category | flops | bytes accessed | tf_op | source)
XLA Modules:
  0.0 220.5 jit_solution(2753661675826970912)
XLA Ops:
  7.2 0.0 copy-start
  7.2 0.0 copy-start.1
  7.2 0.0 all-gather.5.cloned.1.call-start
  7.2 1.0 copy-done
  8.2 0.7 constant_dynamic-slice_fusion
  8.9 0.0 all-gather.5.cloned.1.call-update
  8.9 0.0 all-gather.7.cloned.1.call-start
  9.0 1.2 copy.32
  10.2 0.1 fusion.37
  10.3 0.8 fusion.38
  11.1 66.6 %all-gather.5.cloned.1.call-done = bf16[3072,768]{1,0:T(8,128)(2,1)} async-done(((bf16[96,768]{1,0:T(8,128)(2,1)}), bf16[3072,768]{1,0:T(8,128)(2,1)}) %all-gather.5.cloned.1.call-update) | async-done | bytes 4718608 | tf_op jit(solution)/shard_map/all_gather | solution.py:27
  77.8 0.0 copy-done.1
  77.8 0.0 copy-start.2
  77.8 3.8 %multiply_reduce_fusion = (f32[256]{0:T(256)S(1)}, f32[768,256]{1,0:T(8,128)S(1)}) fusion(bf16[3072,768]{1,0:T(8,128)(2,1)} %all-gather.5.cloned.1.call-done, bf16[1,256,3072]{2,1,0:T(8,128)(2,1)S(1)} %copy-done.1), kind=kOutput, calls=%fused_computation.57 | convolution fusion | flops 1208352512 | bytes 7078912 | tf_op jit(solution)/shard_map/dot_general | solution.py:33
  81.6 0.0 copy-start.4
  81.6 0.1 fusion.55
  81.7 0.0 copy-done.2
  81.7 0.9 pad_maximum_fusion
  82.7 0.0 all-gather.7.cloned.1.call-update
  82.7 0.0 all-gather.9.cloned.1.call-start
  84.0 0.0 copy-done.4
  84.1 8.0 %all-gather = f32[4,1,256]{2,1,0:T(1,128)S(1)} all-gather(f32[1,1,256]{2,1,0:T(1,128)S(1)} %bitcast.120), channel_id=1, replica_groups=mesh['blk'=4,'group'=8] {'blk'}, dimensions={0}, use_global_device_ids=true | all-gather | bytes 5120 | tf_op jit(solution)/shard_map/all_gather | solution.py:40
  92.1 33.4 %all-gather.7.cloned.1.call-done = bf16[2,1024,768]{1,2,0:T(8,128)(2,1)} async-done(((bf16[2,256,768]{1,2,0:T(8,128)(2,1)}), bf16[2,1024,768]{1,2,0:T(8,128)(2,1)}) %all-gather.7.cloned.1.call-update) | async-done | bytes 3145744 | tf_op jit(solution)/shard_map/all_gather | solution.py:37
  125.5 4.6 %fusion.39 = (f32[256]{0:T(256)S(1)}, f32[256,768]{0,1:T(8,128)}) fusion(f32[768,256]{1,0:T(8,128)S(1)} %get-tuple-element.16, f32[256]{0:T(256)S(1)} %add_rsqrt_fusion, bf16[2,1024,768]{1,2,0:T(8,128)(2,1)} %all-gather.7.cloned.1.call-done, f32[]{:T(128)} %bitcast.115, f32[]{:T(128)} %bitcast.112, f32[256]{0:T(256)S(1)} %add_convert_fusion, ...), kind=kOutput, calls=%fused_computation.53 | convolution fusion | flops 809434880 | bytes 5513224 | tf_op jit(solution)/shard_map/dot_general | solution.py:69
  130.1 2.0 fusion.42
  132.1 0.0 all-gather.9.cloned.1.call-update
  132.2 0.0 reduce-scatter.4.cloned.1.call-start
  132.2 1.6 copy.37
  133.8 27.8 %all_to_all.19 = bf16[256,4,768]{0,2,1:T(8,128)(2,1)S(1)} all-to-all(bf16[256,4,768]{0,2,1:T(8,128)(2,1)} %bitcast.117), channel_id=1, replica_groups=mesh['blk'=4,'group'=8] {'blk'}, dimensions={1} | all-to-all | bytes 3145728 | tf_op jit(solution)/shard_map/all_to_all | solution.py:28
  161.6 1.6 copy.38
  163.2 9.1 %all-gather.9.cloned.1.call-done = bf16[1024,768]{0,1:T(8,128)(2,1)} async-done(((bf16[256,768]{0,1:T(8,128)(2,1)}), bf16[1024,768]{0,1:T(8,128)(2,1)}) %all-gather.9.cloned.1.call-update) | async-done | bytes 1572880 | tf_op jit(solution)/shard_map/all_gather | solution.py:86
  172.3 3.3 %convolution_bitcast_fusion = f32[768,768]{0,1:T(8,128)S(1)} fusion(bf16[1024,768]{0,1:T(8,128)(2,1)} %all-gather.9.cloned.1.call-done, bf16[1024,768]{1,0:T(8,128)(2,1)} %bitcast.118), kind=kOutput, calls=%fused_computation.1 | convolution fusion | flops 1207959552 | bytes 5505024 | tf_op jit(solution)/shard_map/dot_general | solution.py:87
  175.5 2.0 copy.43
  177.5 0.0 copy-start.3
  177.5 0.0 reduce-scatter.4.cloned.1.call-update
  177.6 1.0 copy-done.3
  178.5 0.0 copy-start.5
  178.5 3.5 %fusion.25 = (f32[256]{0:T(256)}, f32[256,1024]{1,0:T(8,128)S(1)}) fusion(s32[256]{0:T(256)S(1)} %bitcast.122, f32[]{:T(128)} %bitcast.114, bf16[2,1024,768]{1,2,0:T(8,128)(2,1)} %all-gather.7.cloned.1.call-done, bf16[1,256,768]{1,2,0:T(8,128)(2,1)S(1)} %copy-done.3, f32[]{:T(128)} %bitcast.111), kind=kOutput, calls=%fused_computation.31 | convolution fusion | flops 406060800 | bytes 3017728 | tf_op jit(solution)/shard_map/dot_general | solution.py:47
  182.0 0.0 copy-done.5
  182.0 1.0 fusion.33
  182.9 0.2 fusion.53
  183.1 0.9 copy.39
  184.0 29.9 %reduce-scatter.4.cloned.1.call-done = f32[96,768]{1,0:T(8,128)} async-done(((f32[768,768]{1,0:T(8,128)}), f32[96,768]{1,0:T(8,128)}) %reduce-scatter.4.cloned.1.call-update) | async-done | bytes 294928
  (4 shorter events, 0.0 us)
Async XLA Ops:
  7.2 1.1 copy-start
  7.2 70.6 %copy-start.1 = (bf16[1,256,3072]{2,1,0:T(8,128)(2,1)S(1)}, bf16[1,256,3072]{2,1,0:T(8,128)(2,1)}, u32[]{:S(2)}) copy-start(bf16[1,256,3072]{2,1,0:T(8,128)(2,1)} %param.7) | copy-start | bytes 4718596
  7.2 70.6 %all-gather.5.cloned.1.call-start = ((), (), s32[]{:S(2)}) async-start(), calls=%async_computation.2 | async-start | bytes 4866048 | tf_op jit(solution)/shard_map/all_gather | solution.py:27
  8.9 116.6 %all-gather.7.cloned.1.call-start = ((), (), s32[]{:S(2)}) async-start(), calls=%async_computation.3 | async-start | bytes 3932160 | tf_op jit(solution)/shard_map/all_gather | solution.py:37
  77.8 3.9 %copy-start.2 = (bf16[1,256,768]{1,2,0:T(8,128)(2,1)S(1)}, bf16[1,256,768]{1,2,0:T(8,128)(2,1)}, u32[]{:S(2)}) copy-start(bf16[1,256,768]{1,2,0:T(8,128)(2,1)} %fusion.38) | copy-start | bytes 1179652
  81.6 2.4 %copy-start.4 = (s32[1,256]{1,0:T(1,128)S(1)}, s32[1,256]{1,0:T(1,128)}, u32[]{:S(2)}) copy-start(s32[1,256]{1,0:T(1,128)} %param.9) | copy-start | bytes 3076
  82.7 89.6 %all-gather.9.cloned.1.call-start = ((), (), s32[]{:S(2)}) async-start(), calls=%async_computation.4 | async-start | bytes 1966080 | tf_op jit(solution)/shard_map/all_gather | solution.py:86
  132.2 81.8 %reduce-scatter.4.cloned.1.call-start = ((), (), s32[]{:S(2)}) async-start(), calls=%async_computation.5 | async-start | bytes 2654208
  177.5 1.0 copy-start.3
  178.5 3.5 %copy-start.5 = (bf16[2,1024,768]{1,2,0:T(8,128)(2,1)S(1)}, bf16[2,1024,768]{1,2,0:T(8,128)(2,1)}, u32[]{:S(2)}) copy-start(bf16[2,1024,768]{1,2,0:T(8,128)(2,1)} %all-gather.7.cloned.1.call-done) | copy-start | bytes 9437188
Sparse Core Ops, SparseCore 0:
  11.5 66.2 all-gather.4
  82.8 42.6 all-gather.6
  132.3 39.9 all-gather.8
  177.7 36.2 reduce-scatter.3
where the time goes:
time: 221 us; the launch traced here: 220 us
  waiting for transfers between devices  139 us (63%)
  blocking collectives  35.8 us (16%)
  matrix products  16.1 us (7%)
  between operations  15.2 us (7%)
  local copies, waits for them, and re-layouts  9.92 us (4%)
  other arithmetic  4.17 us (2%)
    all_gather x1, waiting for transfers between devices, body(): w_full = lax.all_gather(w_piece, ('group', 'blk'), axis=0, tiled=True)  66.6 us
    all_gather x1, waiting for transfers between devices, body(): lax.all_gather(jnp.stack([image_unit, text_unit]), 'blk', axis=1, tiled=T...  33.4 us
    unnamed x5, waiting for transfers between devices  30 us
    all_to_all x1, blocking collectives, body(): lax.all_to_all(hidden_rows, 'blk', split_axis=1, concat_axis=0, tiled=True)  27.8 us
    all_gather x1, waiting for transfers between devices, body(): lax.all_gather(projection_output_gradient, 'blk', axis=0, tiled=True)  9.09 us
    all_gather x1, blocking collectives, body(): lax.all_gather(label_rows.astype(jnp.float32), 'blk', axis=0, tiled=True)  8.03 us
    unnamed x16, local copies, waits for them, and re-layouts  7.66 us
    dot_general x1, matrix products, body(): lax.dot_general(weights_of(logits_t, pair_sign_t), image_all, (((0,), (0,...  4.64 us
  transfers between devices with their start and end apart: 4, of which 4 were waited for; matrix products, arithmetic and copies ran while one was open for 5% of the time, Pallas kernels for 0%

commit v1 on v0

--- a/solution.py
+++ b/solution.py
@@ -1,9 +1,23 @@
+import functools
 import jax
 import jax.numpy as jnp
 from jax import lax
 from jax.sharding import PartitionSpec as P
+from jax.lax import all_to_all, axis_size
 
 epsilon = 1e-06
+
+
+def _view_gates(here_x, shard_axis):
+    return jnp.concatenate(
+        all_to_all(
+            jnp.stack(jnp.split(here_x, axis_size(shard_axis), 1), axis=0), shard_axis, 0, 0
+        ),
+        0,
+    )
+
+
+update_task = functools.partial(_view_gates, shard_axis="blk")
 
 
 def body(
@@ -25,7 +39,7 @@
     piece_rows = linear_map_matrix.shape[0] // blocks
     w_piece = lax.dynamic_slice_in_dim(linear_map_matrix, my_index * piece_rows, piece_rows, 0)
     w_full = lax.all_gather(w_piece, ("group", "blk"), axis=0, tiled=True)
-    hidden_chunk = lax.all_to_all(hidden_rows, "blk", split_axis=1, concat_axis=0, tiled=True)
+    hidden_chunk = update_task(hidden_rows)
     image_float = image_rows.astype(jnp.float32)
     image_scale = lax.rsqrt(jnp.sum(image_float * image_float, axis=1, keepdims=True) + epsilon)
     image_dir = image_float * image_scale

time: 221 us -> 220 us (level)
  local copies, waits for them, and re-layouts: 9.92 us -> 4.85 us
  waiting for transfers between devices: 139 us -> 143 us
    unnamed x5 -> x4, waiting for transfers between devices: 30 us -> 0.07 us
    reduce_scatter x0 -> x1, waiting for transfers between devices: none -> 29.9 us  [body(): lax.psum_scatter(partial, 'group', scatter_dimension=0, tiled=True)]
    all_gather x1, waiting for transfers between devices: 9.09 us -> 13 us  [body(): lax.all_gather(projection_output_gradient, 'blk', axis=0, tiled=True)]
    unnamed x16 -> x14, local copies, waits for them, and re-layouts: 7.66 us -> 4.08 us
  transfers between devices with their start and end apart: 4 -> 4, of which waited for: 4 -> 4; matrix products, arithmetic and copies ran while one was open for 5% -> 4% of each run, Pallas kernels for 0% -> 0%
where the time goes in v1:
time: 220 us
  waiting for transfers between devices  143 us (65%)
  blocking collectives  34.7 us (16%)
  matrix products  17.3 us (8%)
  between operations  15.2 us (7%)
  local copies, waits for them, and re-layouts  4.85 us (2%)
  other arithmetic  4.38 us (2%)
    all_gather x1, waiting for transfers between devices, body(): w_full = lax.all_gather(w_piece, ('group', 'blk'), axis=0, tiled=True)  66.6 us
    all_gather x1, waiting for transfers between devices, body(): lax.all_gather(jnp.stack([image_unit, text_unit]), 'blk', axis=1, tiled=T...  33.4 us
    reduce_scatter x1, waiting for transfers between devices, body(): lax.psum_scatter(partial, 'group', scatter_dimension=0, tiled=True)  29.9 us
    all_to_all x1, blocking collectives, _view_gates(): all_to_all(jnp.stack(jnp.split(here_x, axis_size(shard_axis), 1), axis=0)...  26.7 us
    all_gather x1, waiting for transfers between devices, body(): lax.all_gather(projection_output_gradient, 'blk', axis=0, tiled=True)  13 us
    all_gather x1, blocking collectives, body(): lax.all_gather(label_rows.astype(jnp.float32), 'blk', axis=0, tiled=True)  8.03 us
    dot_general x1, matrix products, body(): lax.dot_general(weights_of(logits_t, pair_sign_t), image_all, (((0,), (0,...  4.7 us
  transfers between devices with their start and end apart: 4, of which 4 were waited for; matrix products, arithmetic and copies ran while one was open for 4% of the time, Pallas kernels for 0%

profile of v1, /device:TPU:0, one launch (start us, length us, event | category | flops | bytes accessed | tf_op | source)
XLA Modules:
  0.0 219.6 jit_solution(5348522946042424322)
XLA Ops:
  7.2 0.0 copy-start
  7.2 0.0 copy-start.1
  7.2 0.0 all-gather.5.cloned.1.call-start
  7.2 1.0 copy-done
  8.2 0.7 constant_dynamic-slice_fusion
  8.9 0.0 all-gather.5.cloned.1.call-update
  8.9 0.0 all-gather.7.cloned.1.call-start
  9.0 1.2 copy.15
  10.2 0.1 fusion.35
  10.3 0.8 fusion.36
  11.1 66.6 %all-gather.5.cloned.1.call-done = bf16[3072,768]{1,0:T(8,128)(2,1)} async-done(((bf16[96,768]{1,0:T(8,128)(2,1)}), bf16[3072,768]{1,0:T(8,128)(2,1)}) %all-gather.5.cloned.1.call-update) | async-done | bytes 4718608 | tf_op jit(solution)/shard_map/all_gather | solution.py:41
  77.8 0.0 copy-done.1
  77.8 0.0 copy-start.2
  77.8 3.8 %multiply_reduce_fusion = (f32[256]{0:T(256)S(1)}, f32[768,256]{1,0:T(8,128)S(1)}) fusion(bf16[3072,768]{1,0:T(8,128)(2,1)} %all-gather.5.cloned.1.call-done, bf16[1,256,3072]{2,1,0:T(8,128)(2,1)S(1)} %copy-done.1), kind=kOutput, calls=%fused_computation.55 | convolution fusion | flops 1208352512 | bytes 7078912 | tf_op jit(solution)/shard_map/dot_general | solution.py:47
  81.6 0.0 copy-start.4
  81.6 0.1 fusion.53
  81.7 0.0 copy-done.2
  81.7 0.9 pad_maximum_fusion.1
  82.7 0.0 all-gather.7.cloned.1.call-update
  82.7 0.0 all-gather.9.cloned.1.call-start
  84.0 0.0 copy-done.4
  84.1 8.0 %all-gather = f32[4,1,256]{2,1,0:T(1,128)S(1)} all-gather(f32[1,1,256]{2,1,0:T(1,128)S(1)} %bitcast.122), channel_id=1, replica_groups=mesh['blk'=4,'group'=8] {'blk'}, dimensions={0}, use_global_device_ids=true | all-gather | bytes 5120 | tf_op jit(solution)/shard_map/all_gather | solution.py:54
  92.1 33.4 %all-gather.7.cloned.1.call-done = bf16[2,1024,768]{1,2,0:T(8,128)(2,1)} async-done(((bf16[2,256,768]{1,2,0:T(8,128)(2,1)}), bf16[2,1024,768]{1,2,0:T(8,128)(2,1)}) %all-gather.7.cloned.1.call-update) | async-done | bytes 3145744 | tf_op jit(solution)/shard_map/all_gather | solution.py:51
  125.5 4.7 %fusion.37 = (f32[256]{0:T(256)S(1)}, f32[256,768]{0,1:T(8,128)}) fusion(f32[768,256]{1,0:T(8,128)S(1)} %get-tuple-element.14, f32[256]{0:T(256)S(1)} %add_rsqrt_fusion, bf16[2,1024,768]{1,2,0:T(8,128)(2,1)} %all-gather.7.cloned.1.call-done, f32[]{:T(128)} %bitcast.118, f32[]{:T(128)} %bitcast.115, f32[256]{0:T(256)S(1)} %add_convert_fusion, ...), kind=kOutput, calls=%fused_computation.51 | convolution fusion | flops 809434880 | bytes 5513224 | tf_op jit(solution)/shard_map/dot_general | solution.py:83
  130.2 2.0 fusion.40
  132.2 0.0 all-gather.9.cloned.1.call-update
  132.2 0.0 reduce-scatter.2.cloned.1.call-start
  132.3 0.1 slice_bitcast_fusion.35
  132.4 0.2 pad_maximum_fusion
  132.6 26.7 %all_to_all.5 = bf16[4,256,768]{2,1,0:T(8,128)(2,1)S(1)} all-to-all(bf16[4,256,768]{2,1,0:T(8,128)(2,1)S(1)} %pad_maximum_fusion), channel_id=1, replica_groups=mesh['blk'=4,'group'=8] {'blk'}, dimensions={0} | all-to-all | bytes 3145728 | tf_op jit(solution)/shard_map/all_to_all | solution.py:13
  159.3 13.0 %all-gather.9.cloned.1.call-done = bf16[1024,768]{0,1:T(8,128)(2,1)} async-done(((bf16[256,768]{0,1:T(8,128)(2,1)}), bf16[1024,768]{0,1:T(8,128)(2,1)}) %all-gather.9.cloned.1.call-update) | async-done | bytes 1572880 | tf_op jit(solution)/shard_map/all_gather | solution.py:100
  172.3 4.3 %fusion.60 = f32[768,768]{1,0:T(8,128)} fusion(bf16[1024,768]{1,0:T(8,128)(2,1)S(1)} %bitcast.120, bf16[1024,768]{0,1:T(8,128)(2,1)} %all-gather.9.cloned.1.call-done), kind=kOutput, calls=%fused_computation.83 | convolution fusion | flops 1207959552 | bytes 5505024 | tf_op jit(solution)/shard_map/dot_general | solution.py:101
  176.6 0.0 copy-start.3
  176.6 0.0 reduce-scatter.2.cloned.1.call-update
  176.7 1.0 copy-done.3
  177.6 0.0 copy-start.5
  177.6 3.5 %fusion.23 = (f32[256]{0:T(256)}, f32[256,1024]{1,0:T(8,128)S(1)}) fusion(s32[256]{0:T(256)S(1)} %bitcast.124, f32[]{:T(128)} %bitcast.117, bf16[2,1024,768]{1,2,0:T(8,128)(2,1)} %all-gather.7.cloned.1.call-done, bf16[1,256,768]{1,2,0:T(8,128)(2,1)S(1)} %copy-done.3, f32[]{:T(128)} %bitcast.114), kind=kOutput, calls=%fused_computation.29 | convolution fusion | flops 406060800 | bytes 3017728 | tf_op jit(solution)/shard_map/dot_general | solution.py:61
  181.1 0.0 copy-done.5
  181.1 1.0 fusion.31
  182.1 0.1 fusion.51
  182.2 0.9 copy.20
  183.1 29.9 %reduce-scatter.2.cloned.1.call-done = f32[96,768]{1,0:T(8,128)} async-done(((f32[768,768]{1,0:T(8,128)}), f32[96,768]{1,0:T(8,128)}) %reduce-scatter.2.cloned.1.call-update) | async-done | bytes 294928 | tf_op jit(solution)/shard_map/reduce_scatter | solution.py:104
  (4 shorter events, 0.0 us)
Async XLA Ops:
  7.2 1.1 copy-start
  7.2 70.6 %copy-start.1 = (bf16[1,256,3072]{2,1,0:T(8,128)(2,1)S(1)}, bf16[1,256,3072]{2,1,0:T(8,128)(2,1)}, u32[]{:S(2)}) copy-start(bf16[1,256,3072]{2,1,0:T(8,128)(2,1)} %param.7) | copy-start | bytes 4718596
  7.2 70.6 %all-gather.5.cloned.1.call-start = ((), (), s32[]{:S(2)}) async-start(), calls=%async_computation.2 | async-start | bytes 4866048 | tf_op jit(solution)/shard_map/all_gather | solution.py:41
  8.9 116.6 %all-gather.7.cloned.1.call-start = ((), (), s32[]{:S(2)}) async-start(), calls=%async_computation.3 | async-start | bytes 3932160 | tf_op jit(solution)/shard_map/all_gather | solution.py:51
  77.8 4.0 %copy-start.2 = (bf16[1,256,768]{1,2,0:T(8,128)(2,1)S(1)}, bf16[1,256,768]{1,2,0:T(8,128)(2,1)}, u32[]{:S(2)}) copy-start(bf16[1,256,768]{1,2,0:T(8,128)(2,1)} %fusion.36) | copy-start | bytes 1179652
  81.6 2.4 %copy-start.4 = (s32[1,256]{1,0:T(1,128)S(1)}, s32[1,256]{1,0:T(1,128)}, u32[]{:S(2)}) copy-start(s32[1,256]{1,0:T(1,128)} %param.9) | copy-start | bytes 3076
  82.7 89.7 %all-gather.9.cloned.1.call-start = ((), (), s32[]{:S(2)}) async-start(), calls=%async_computation.4 | async-start | bytes 1966080 | tf_op jit(solution)/shard_map/all_gather | solution.py:100
  132.2 80.8 %reduce-scatter.2.cloned.1.call-start = ((), (), s32[]{:S(2)}) async-start(), calls=%async_computation.5 | async-start | bytes 2654208 | tf_op jit(solution)/shard_map/reduce_scatter | solution.py:104
  176.6 1.0 copy-start.3
  177.6 3.5 %copy-start.5 = (bf16[2,1024,768]{1,2,0:T(8,128)(2,1)S(1)}, bf16[2,1024,768]{1,2,0:T(8,128)(2,1)}, u32[]{:S(2)}) copy-start(bf16[2,1024,768]{1,2,0:T(8,128)(2,1)} %all-gather.7.cloned.1.call-done) | copy-start | bytes 9437188
Sparse Core Ops, SparseCore 0:
  11.5 66.2 all-gather.4
  82.8 42.6 all-gather.6
  132.4 39.9 all-gather.8
  176.8 36.2 reduce-scatter.1
